TPU v7x, 512 devices: a whole 4x8x8 slice. The times are simulated.
512 devices in a mesh: blk: 16 (over x_lo, y), exp: 32 (over z, x_hi, core).
Axes of the slice: x: 4 (x_hi: 2, x_lo: 2; x = x_hi * 2 + x_lo), y: 8, z: 8, core: 2. Of those that a mesh axis runs over, the one named last changes fastest.
Arguments:
- residual: bfloat16 [32, 2048, 1024], P('exp', 'blk'), may hold values from -6 to 6
- queries: bfloat16 [32, 2048, 1024], P('exp', 'blk'), may hold values from -6 to 6
- suffix_kv: bfloat16 [32, 2048, 1024], P('exp', 'blk'), may hold values from -6 to 6
- prompt_kv: bfloat16 [32, 1024, 1024], P('exp', 'blk'), may hold values from -6 to 6
- prompt_lengths: int32 [32], P('exp'), may hold values from 1 to 1024, as said below
- block_keep: int32 [32, 32], P('exp', 'blk'), may hold values 0 or 1
- suffix_lengths: int32 [32, 16, 4], P('exp', 'blk'), may hold values from 1 to 64, 128 in all within a row
- out_weight: bfloat16 [1024, 1024], P('exp'), may hold values from -0.75 to 0.75
- routes: int32 [32, 2048, 8], P('exp', 'blk'), may hold values from 0 to 31, all different within a row; in each aligned block of 128 rows (0 to 127, 128 to 255, ..., all dimensions but the last counted through in order) at most 40 rows name the same one
- route_weight: float32 [32, 2048, 8], P('exp', 'blk'), may hold values from 0.02 to 0.25
- gate_up_weight: bfloat16 [32, 1024, 1024], P('exp'), may hold values from -0.1875 to 0.1875
- down_weight: bfloat16 [32, 512, 1024], P('exp'), may hold values from -0.25 to 0.25
- page_owner: int32 [32, 128, 1], P('exp', 'blk'), may hold values from 0 to 15; in each aligned block of 8 rows (0 to 7, 8 to 15, ..., all dimensions but the last counted through in order) at most 2 rows name the same one
Outputs:
- attended: bfloat16 [32, 2048, 1024], P('exp', 'blk')
- layer_out: bfloat16 [32, 2048, 1024], P('exp', 'blk')
- cache_pages: bfloat16 [32, 4096, 1024], P('exp', 'blk')
Inputs may be any that keep to these rules, and one draw needn't show every extreme that they name: `prompt_lengths`: some group's prompt length equals 1024. `suffix_lengths`: each device's 4 request lengths sum to 128. `routes`: each token names 8 different experts; among the tokens of one device at most 40 name any one expert, and that bound is reached. `page_owner`: among the 8 pages of one device at most 2 go to any one owner, and that bound is reached.
All inputs are finite; a program needn't handle non-finite values. No bound on the sum of `block_keep` on one device may be relied on, other than what follows from the above.
Results may differ from a plain program's by a relative error of at most 0.013.
Values may be sent and summed in bfloat16 or wider, within the bound.
No kernel may reach another device: no remote copies, remote signals or barrier semaphores. Data moves between devices by JAX's collectives and lax.ppermute only.
A program may use at most 64 MiB of HBM per device.

v0:
```python
import jax
import jax.numpy as jnp
from jax import lax
from jax.sharding import PartitionSpec as P

D = 1024
H = 16
KVH = 8
HD = 64
FF = 512
TOPK = 8
EXP_DEV = 1
KB = 32
PAGE = 8
SCALE = 0.125
NEGATIVE = -1e30
EPSILON = 1e-06


def segment_of(lengths, count):
    ends = jnp.cumsum(lengths)
    position = jnp.arange(count, dtype=jnp.int32)
    return jnp.sum((position[:, None] >= ends[None, :]).astype(jnp.int32), axis=1)


def rank_within(labels, count):
    onehot = (labels[:, None] == jnp.arange(count, dtype=jnp.int32)[None, :]).astype(jnp.int32)
    before = jnp.cumsum(onehot, axis=0) - onehot
    return jnp.sum(before * onehot, axis=1)


def absorb(carry_state, query_heads, key_heads, value_heads, visible):
    running_max, denom, numerator = carry_state
    scores = (
        jnp.einsum("tkgd,skd->tkgs", query_heads, key_heads, preferred_element_type=jnp.float32)
        * SCALE
    )
    new_max = jnp.maximum(running_max, jnp.max(jnp.where(visible, scores, NEGATIVE), axis=-1))
    factor = jnp.exp(running_max - new_max)
    weight = jnp.where(visible, jnp.exp(scores - new_max[..., None]), 0.0)
    denom = denom * factor + jnp.sum(weight, axis=-1)
    added = jnp.einsum(
        "tkgs,skd->tkgd",
        weight.astype(jnp.bfloat16),
        value_heads,
        preferred_element_type=jnp.float32,
    )
    numerator = numerator * factor[..., None] + added
    return (new_max, denom, numerator)


def local(
    residual,
    queries,
    suffix_kv,
    prompt_kv,
    prompt_lengths,
    block_keep,
    suffix_lengths,
    out_weight,
    routes,
    route_weight,
    gate_up_weight,
    down_weight,
    page_owner,
):
    tok_rows = queries.shape[1]
    kv_width = suffix_kv.shape[2] // 2
    group_size = H // KVH
    query_heads = queries[0].reshape(tok_rows, KVH, group_size, HD)
    own_keys = suffix_kv[0, :, :kv_width].reshape(tok_rows, KVH, HD)
    own_values = suffix_kv[0, :, kv_width:].reshape(tok_rows, KVH, HD)
    segment = segment_of(suffix_lengths[0, 0], tok_rows)
    position = jnp.arange(tok_rows, dtype=jnp.int32)
    own_seen = ((segment[:, None] == segment[None, :]) & (position[None, :] <= position[:, None]))[
        :, None, None, :
    ]
    start_state = (
        jnp.full((tok_rows, KVH, group_size), NEGATIVE, jnp.float32),
        jnp.zeros((tok_rows, KVH, group_size), jnp.float32),
        jnp.zeros((tok_rows, KVH, group_size, HD), jnp.float32),
    )
    carry_state = absorb(start_state, query_heads, own_keys, own_values, own_seen)
    block_rows = prompt_kv.shape[1]
    keep_rows = jnp.repeat(block_keep[0], KB)
    position_abs = lax.axis_index("blk") * block_rows + jnp.arange(block_rows, dtype=jnp.int32)
    live_keys = ((keep_rows > 0) & (position_abs < prompt_lengths[0])).astype(jnp.int32)[None, :]
    piece_kv = lax.all_gather(prompt_kv, "blk", axis=1, tiled=True)
    piece_live = lax.all_gather(live_keys, "blk", axis=1, tiled=True)
    count = piece_kv.shape[1]
    key_heads = piece_kv[0, :, :kv_width].reshape(count, KVH, HD)
    value_heads = piece_kv[0, :, kv_width:].reshape(count, KVH, HD)
    visible = (piece_live[0] > 0)[None, None, None, :]
    running_max, denom, numerator = absorb(
        carry_state, query_heads, key_heads, value_heads, visible
    )
    attended = (numerator / denom[..., None]).reshape(tok_rows, H * HD).astype(jnp.bfloat16)
    projected = jnp.dot(
        attended,
        lax.all_gather(out_weight, "exp", axis=0, tiled=True),
        preferred_element_type=jnp.float32,
    )
    stream = (residual[0].astype(jnp.float32) + projected).astype(jnp.bfloat16)
    stream_f32 = stream.astype(jnp.float32)
    normed = (
        stream_f32 * lax.rsqrt(jnp.mean(stream_f32 * stream_f32, axis=-1, keepdims=True) + EPSILON)
    ).astype(jnp.bfloat16)
    exp_count = lax.axis_size("exp")
    experts = EXP_DEV * exp_count
    capacity = min(tok_rows, 5 * tok_rows * TOPK // (4 * experts))
    flat_routes = routes[0].reshape(-1)
    slot_index = flat_routes * capacity + rank_within(flat_routes, experts)
    dispatch = (
        jnp.zeros((experts * capacity, D), jnp.bfloat16)
        .at[slot_index]
        .set(jnp.repeat(normed, TOPK, axis=0))
    )
    dispatch = dispatch.reshape(experts, capacity, D)
    arrived = lax.all_to_all(dispatch, "exp", split_axis=0, concat_axis=0, tiled=True)
    count = arrived.shape[1]
    grouped = arrived.reshape(exp_count, EXP_DEV, count, D)
    picked_rows = grouped[:, 0].reshape(exp_count * count, D)
    gate_up = jnp.dot(picked_rows, gate_up_weight[0], preferred_element_type=jnp.float32)
    hidden = (jax.nn.silu(gate_up[:, :FF]) * gate_up[:, FF:]).astype(jnp.bfloat16)
    result = jnp.dot(hidden, down_weight[0], preferred_element_type=jnp.float32).astype(
        jnp.bfloat16
    )
    results = [result.reshape(exp_count, count, D)]
    outgoing = jnp.stack(results, axis=1).reshape(exp_count * EXP_DEV, count, D)
    returned = lax.all_to_all(outgoing, "exp", split_axis=0, concat_axis=0, tiled=True)
    picked = (
        returned.reshape(experts * capacity, D)[slot_index]
        .astype(jnp.float32)
        .reshape(tok_rows, TOPK, D)
    )
    layer_out = (stream_f32 + jnp.sum(picked * route_weight[0][:, :, None], axis=1)).astype(
        jnp.bfloat16
    )
    page_count = block_rows // PAGE
    blk_count = lax.axis_size("blk")
    page_capacity = max(2, 2 * page_count // blk_count)
    page_rows = prompt_kv[0].reshape(page_count, PAGE, 2 * kv_width)
    owners = page_owner[0, :, 0]
    page_slot = owners * page_capacity + rank_within(owners, blk_count)
    outgoing_pages = (
        jnp.zeros((blk_count * page_capacity, PAGE, 2 * kv_width), jnp.bfloat16)
        .at[page_slot]
        .set(page_rows)
    )
    arrived_pages = lax.all_to_all(outgoing_pages, "blk", split_axis=0, concat_axis=0, tiled=True)
    cache_pages = arrived_pages.reshape(1, blk_count * page_capacity * PAGE, 2 * kv_width)
    return (attended[None], layer_out[None], cache_pages)


def solution(mesh):
    return jax.shard_map(
        local,
        mesh=mesh,
        in_specs=(
            P("exp", "blk", None),
            P("exp", "blk", None),
            P("exp", "blk", None),
            P("exp", "blk", None),
            P("exp"),
            P("exp", "blk"),
            P("exp", "blk", None),
            P("exp", None),
            P("exp", "blk", None),
            P("exp", "blk", None),
            P("exp", None, None),
            P("exp", None, None),
            P("exp", "blk", None),
        ),
        out_specs=(P("exp", "blk", None), P("exp", "blk", None), P("exp", "blk", None)),
        check_vma=False,
    )
```

profile of v0, /device:TPU:1, one launch (start us, length us, event | category | flops | bytes accessed | tf_op | source)
XLA Modules:
  0.0 363.6 jit_solution(11211758966048198514)
XLA Ops:
  9.4 0.8 copy.48
  11.6 1.0 fusion.51
  12.7 0.8 reduce-window.18
  13.6 9.0 %reduce-window.19 = s32[32,8,128]{2,1,0:T(8,128)S(1)} reduce-window(s32[32,8,128]{2,1,0:T(8,128)S(1)} %fusion.39, s32[]{:T(128)} %constant.17.clone.1), window={size=1x1x128 pad=0_0x0_0x127_0}, to_apply=%region_6.7 | reduce-window | flops 4161536 | bytes 262148 | tf_op jit(solution)/shard_map/reduce-window.1
  23.0 1.3 dynamic-slice
  25.2 1.1 copy.41
  26.8 15.1 %all-reduce = s32[1024]{0:T(1024)S(1)} all-reduce(s32[1024]{0:T(1024)S(1)} %fusion.43), channel_id=1, replica_groups=mesh['blk'=16,'exp'=32] {'blk'}, use_global_device_ids=true, to_apply=%add | all-reduce | flops 1024 | bytes 8192
  43.3 1.9 select_reduce_fusion
  45.2 35.0 %all-gather.3.cloned.1.call-done = bf16[1,1024,1024]{2,1,0:T(8,128)(2,1)} async-done(((bf16[1,64,1024]{2,1,0:T(8,128)(2,1)}), bf16[1,1024,1024]{2,1,0:T(8,128)(2,1)}) %all-gather.3.cloned.1.call-update) | async-done | bytes 2097168 | tf_op jit(solution)/shard_map/all_gather | solution.py:88
  80.2 2.7 fusion.50
  82.9 1.3 copy.45
  84.2 1.5 copy.44
  85.7 2.9 fusion
  89.0 2.2 fusion.3
  91.2 1.5 fusion.17
  93.1 84.1 %all-gather.5.cloned.1.call-done = bf16[1024,1024]{1,0:T(8,128)(2,1)} async-done(((bf16[32,1024]{1,0:T(8,128)(2,1)}), bf16[1024,1024]{1,0:T(8,128)(2,1)}) %all-gather.5.cloned.1.call-update) | async-done | bytes 2097168 | tf_op jit(solution)/shard_map/all_gather | solution.py:100
  177.2 2.1 multiply_reduce_fusion
  179.5 7.1 %scatter_custom_fusion = bf16[1280,1024]{1,0:T(8,128)(2,1)} fusion(s32[1024]{0:T(1024)S(1)} %bitcast.143, bf16[]{:T(256)} %constant.12.clone.1, bf16[128,1024]{1,0:T(8,128)(2,1)S(1)} %multiply_convert_fusion), kind=kCustom, calls=%fused_computation.19 | custom fusion | bytes 2883586 | tf_op jit(solution)/shard_map/scatter | solution.py:116
  186.6 4.8 %all-to-all-start = ((bf16[32,40,1024]{2,1,0:T(8,128)(2,1)}), bf16[32,40,1024]{2,1,0:T(8,128)(2,1)}, u32[]{:S(2)}, u32[]{:S(2)}) async-start(bf16[32,40,1024]{2,1,0:T(8,128)(2,1)} %bitcast.128), calls=%async_computation | async-start | bytes 5242880 | tf_op jit(solution)/shard_map/all_to_all | solution.py:119
  191.7 0.9 broadcast_in_dim.91
  192.5 2.1 scatter_fusion
  194.6 57.8 %all-to-all-done = bf16[32,40,1024]{2,1,0:T(8,128)(2,1)} async-done(((bf16[32,40,1024]{2,1,0:T(8,128)(2,1)}), bf16[32,40,1024]{2,1,0:T(8,128)(2,1)}, u32[]{:S(2)}, u32[]{:S(2)}) %all-to-all-start) | async-done | bytes 2621472 | tf_op jit(solution)/shard_map/all_to_all | solution.py:119
  252.4 7.4 %all-to-all-start.2 = ((bf16[32,8,1024]{2,1,0:T(8,128)(2,1)}), bf16[32,8,1024]{2,1,0:T(8,128)(2,1)S(1)}, u32[]{:S(2)}, u32[]{:S(2)}) async-start(bf16[32,8,1024]{2,1,0:T(8,128)(2,1)} %scatter_fusion), calls=%async_computation.2 | async-start | bytes 1048576 | tf_op jit(solution)/shard_map/all_to_all | solution.py:150
  259.8 4.7 %fusion.10 = f32[1280,1024]{1,0:T(8,128)S(1)} fusion(bf16[1280,1024]{1,0:T(8,128)(2,1)} %bitcast.32, bf16[1,1024,1024]{2,1,0:T(8,128)(2,1)S(1)} %copy-done), kind=kOutput, calls=%fused_computation.17 | convolution fusion | flops 2684354560 | bytes 9961472 | tf_op jit(solution)/shard_map/dot_general | solution.py:123
  264.6 3.1 convolution_convert_fusion
  267.7 5.3 %all-to-all-done.2 = bf16[32,8,1024]{2,1,0:T(8,128)(2,1)S(1)} async-done(((bf16[32,8,1024]{2,1,0:T(8,128)(2,1)}), bf16[32,8,1024]{2,1,0:T(8,128)(2,1)S(1)}, u32[]{:S(2)}, u32[]{:S(2)}) %all-to-all-start.2) | async-done | bytes 524320 | tf_op jit(solution)/shard_map/all_to_all | solution.py:150
  273.0 10.2 %all-to-all-start.1 = ((bf16[32,40,1024]{2,1,0:T(8,128)(2,1)}), bf16[32,40,1024]{2,1,0:T(8,128)(2,1)}, u32[]{:S(2)}, u32[]{:S(2)}) async-start(bf16[32,40,1024]{2,1,0:T(8,128)(2,1)} %bitcast.130), calls=%async_computation.1 | async-start | bytes 5242880 | tf_op jit(solution)/shard_map/all_to_all | solution.py:130
  283.3 0.9 copy.53
  284.1 60.0 %all-to-all-done.1 = bf16[32,40,1024]{2,1,0:T(8,128)(2,1)} async-done(((bf16[32,40,1024]{2,1,0:T(8,128)(2,1)}), bf16[32,40,1024]{2,1,0:T(8,128)(2,1)}, u32[]{:S(2)}, u32[]{:S(2)}) %all-to-all-start.1) | async-done | bytes 2621472 | tf_op jit(solution)/shard_map/all_to_all | solution.py:130
  344.2 8.1 %gather_fusion = bf16[1024,1024]{1,0:T(8,128)(2,1)} fusion(bf16[1280,1024]{1,0:T(8,128)(2,1)} %bitcast.36, s32[1024]{0:T(1024)S(1)} %broadcast_clamp_fusion), kind=kCustom, calls=%fused_computation | custom fusion | bytes 4198400 | tf_op jit(solution)/shard_map/gather | solution.py:132
  352.3 2.9 fusion.5
  356.0 0.8 copy.66
  (63 shorter events, 7.4 us)
Async XLA Ops:
  7.2 252.6 %copy-start = (bf16[1,1024,1024]{2,1,0:T(8,128)(2,1)S(1)}, bf16[1,1024,1024]{2,1,0:T(8,128)(2,1)}, u32[]{:S(2)}) copy-start(bf16[1,1024,1024]{2,1,0:T(8,128)(2,1)} %param.23) | copy-start | bytes 6291460
  7.2 73.0 %all-gather.3.cloned.1.call-start = ((), (), s32[]{:S(2)}) async-start(), calls=%async_computation.3 | async-start | bytes 2228224 | tf_op jit(solution)/shard_map/all_gather | solution.py:88
  7.9 169.3 %all-gather.5.cloned.1.call-start = ((), (), s32[]{:S(2)}) async-start(), calls=%async_computation.4 | async-start | bytes 2162688 | tf_op jit(solution)/shard_map/all_gather | solution.py:100
  85.7 3.0 copy-start.5
  85.7 3.0 copy-start.1
  85.7 3.2 copy-start.7
  88.9 2.2 copy-start.2
  92.7 84.5 %copy-start.4 = (bf16[1,128,1024]{2,1,0:T(8,128)(2,1)S(1)}, bf16[1,128,1024]{2,1,0:T(8,128)(2,1)}, u32[]{:S(2)}) copy-start(bf16[1,128,1024]{2,1,0:T(8,128)(2,1)} %param.13) | copy-start | bytes 786436
  93.0 86.4 %copy-start.6 = (s32[1024,1]{0,1:T(1,128)S(1)}, s32[1024,1]{0,1:T(1,128)}, u32[]{:S(2)}) copy-start(s32[1024,1]{0,1:T(1,128)} %compare_select_fusion) | copy-start | bytes 12292
  186.6 4.8 %copy-start.9 = (s32[1,8,1]{1,2,0:T(1,128)S(1)}, s32[1,8,1]{1,2,0:T(1,128)}, u32[]{:S(2)}) copy-start(s32[1,8,1]{1,2,0:T(1,128)} %param.25) | copy-start | bytes 100
  186.6 5.9 %copy-start.3 = (bf16[1,64,1024]{2,1,0:T(8,128)(2,1)S(1)}, bf16[1,64,1024]{2,1,0:T(8,128)(2,1)}, u32[]{:S(2)}) copy-start(bf16[1,64,1024]{2,1,0:T(8,128)(2,1)} %param.16) | copy-start | bytes 393220
  186.6 65.8 %all-to-all-start = ((bf16[32,40,1024]{2,1,0:T(8,128)(2,1)}), bf16[32,40,1024]{2,1,0:T(8,128)(2,1)}, u32[]{:S(2)}, u32[]{:S(2)}) async-start(bf16[32,40,1024]{2,1,0:T(8,128)(2,1)} %bitcast.128), calls=%async_computation | async-start | bytes 5242880 | tf_op jit(solution)/shard_map/all_to_all | solution.py:119
  252.4 20.6 %all-to-all-start.2 = ((bf16[32,8,1024]{2,1,0:T(8,128)(2,1)}), bf16[32,8,1024]{2,1,0:T(8,128)(2,1)S(1)}, u32[]{:S(2)}, u32[]{:S(2)}) async-start(bf16[32,8,1024]{2,1,0:T(8,128)(2,1)} %scatter_fusion), calls=%async_computation.2 | async-start | bytes 1048576 | tf_op jit(solution)/shard_map/all_to_all | solution.py:150
  259.8 4.8 %copy-start.10 = (bf16[1,512,1024]{2,1,0:T(8,128)(2,1)S(1)}, bf16[1,512,1024]{2,1,0:T(8,128)(2,1)}, u32[]{:S(2)}) copy-start(bf16[1,512,1024]{2,1,0:T(8,128)(2,1)} %param.24) | copy-start | bytes 3145732
  273.0 10.2 %copy-start.8 = (f32[1,128,8]{1,2,0:T(8,128)S(1)}, f32[1,128,8]{1,2,0:T(8,128)}, u32[]{:S(2)}) copy-start(f32[1,128,8]{1,2,0:T(8,128)} %param.22) | copy-start | bytes 12292
  273.0 71.2 %all-to-all-start.1 = ((bf16[32,40,1024]{2,1,0:T(8,128)(2,1)}), bf16[32,40,1024]{2,1,0:T(8,128)(2,1)}, u32[]{:S(2)}, u32[]{:S(2)}) async-start(bf16[32,40,1024]{2,1,0:T(8,128)(2,1)} %bitcast.130), calls=%async_computation.1 | async-start | bytes 5242880 | tf_op jit(solution)/shard_map/all_to_all | solution.py:130
Sparse Core Ops, SparseCore 0:
  10.1 70.0 all-gather.2
  83.6 93.5 all-gather.4
where the time goes:
time: 364 us
  waiting for transfers between devices  244 us (67%)
  local copies, waits for them, and re-layouts  30.7 us (8%)
  starting transfers between devices  22.4 us (6%)
  other arithmetic  19.4 us (5%)
  matrix products  16.7 us (5%)
  between operations  15.7 us (4%)
  blocking collectives  15.1 us (4%)
    all_gather x1, waiting for transfers between devices, local(): lax.all_gather(out_weight, 'exp', axis=0, tiled=True)  84.1 us
    all_to_all x1, waiting for transfers between devices, local(): lax.all_to_all(outgoing, 'exp', split_axis=0, concat_axis=0, tiled=True)  60 us
    all_to_all x1, waiting for transfers between devices, local(): lax.all_to_all(dispatch, 'exp', split_axis=0, concat_axis=0, tiled=True)  57.8 us
    all_gather x1, waiting for transfers between devices, local(): piece_kv = lax.all_gather(prompt_kv, 'blk', axis=1, tiled=True)  35 us
    unnamed x1, blocking collectives  15.1 us
    all_to_all x1, starting transfers between devices, local(): lax.all_to_all(outgoing, 'exp', split_axis=0, concat_axis=0, tiled=True)  10.2 us
    another operation x4, other arithmetic  9.95 us
    gather x1, local copies, waits for them, and re-layouts, local(): returned.reshape(experts * capacity, D)[slot_index].astype(jnp.float32)  8.11 us
  transfers between devices with their start and end apart: 5, of which 5 were waited for; matrix products, arithmetic and copies ran while one was open for 12% of the time, Pallas kernels for 0%

commit v1 on v0

--- a/solution.py
+++ b/solution.py
@@ -97,7 +97,9 @@
     attended = (numerator / denom[..., None]).reshape(tok_rows, H * HD).astype(jnp.bfloat16)
     projected = jnp.dot(
         attended,
-        lax.all_gather(out_weight, "exp", axis=0, tiled=True),
+        jnp.concatenate(
+            lax.all_to_all(jnp.stack([out_weight] * lax.axis_size("exp")), "exp", 0, 0), axis=0
+        ),
         preferred_element_type=jnp.float32,
     )
     stream = (residual[0].astype(jnp.float32) + projected).astype(jnp.bfloat16)

time: 364 us -> 295 us (0.81)
  waiting for transfers between devices: 244 us -> 150 us
  starting transfers between devices: 22.4 us -> 48.1 us
    all_gather x1 -> x0, waiting for transfers between devices: 84.1 us -> none  [local(): lax.all_gather(out_weight, 'exp', axis=0, tiled=True)]
    all_to_all x1, starting transfers between devices: 4.77 us -> 19.4 us  [local(): lax.all_to_all(dispatch, 'exp', split_axis=0, concat_axis=0, tiled=True)]
    all_to_all x0 -> x1, starting transfers between devices: none -> 14.6 us  [local(): lax.all_to_all(jnp.stack([out_weight] * lax.axis_size('exp')), 'exp', 0, 0)]
    all_gather x1, waiting for transfers between devices: 35 us -> 26.5 us  [local(): piece_kv = lax.all_gather(prompt_kv, 'blk', axis=1, tiled=True)]
  transfers between devices with their start and end apart: 5 -> 5, of which waited for: 5 -> 4; matrix products, arithmetic and copies ran while one was open for 12% -> 15% of each run, Pallas kernels for 0% -> 0%
where the time goes in v1:
time: 295 us; the launch traced here: 294 us
  waiting for transfers between devices  150 us (51%)
  starting transfers between devices  48.1 us (16%)
  local copies, waits for them, and re-layouts  32 us (11%)
  other arithmetic  17.4 us (6%)
  matrix products  16.8 us (6%)
  between operations  15.7 us (5%)
  blocking collectives  14 us (5%)
    all_to_all x1, waiting for transfers between devices, local(): lax.all_to_all(outgoing, 'exp', split_axis=0, concat_axis=0, tiled=True)  60 us
    all_to_all x1, waiting for transfers between devices, local(): lax.all_to_all(dispatch, 'exp', split_axis=0, concat_axis=0, tiled=True)  57.8 us
    all_gather x1, waiting for transfers between devices, local(): piece_kv = lax.all_gather(prompt_kv, 'blk', axis=1, tiled=True)  26.5 us
    all_to_all x1, starting transfers between devices, local(): lax.all_to_all(dispatch, 'exp', split_axis=0, concat_axis=0, tiled=True)  19.4 us
    all_to_all x1, starting transfers between devices, local(): lax.all_to_all(jnp.stack([out_weight] * lax.axis_size('exp')), 'exp', 0, 0)  14.6 us
    unnamed x1, blocking collectives  14 us
    all_to_all x1, starting transfers between devices, local(): lax.all_to_all(outgoing, 'exp', split_axis=0, concat_axis=0, tiled=True)  10.1 us
    another operation x4, other arithmetic  9.32 us
  transfers between devices with their start and end apart: 5, of which 4 were waited for; matrix products, arithmetic and copies ran while one was open for 15% of the time, Pallas kernels for 0%

profile of v1, /device:TPU:1, one launch (start us, length us, event | category | flops | bytes accessed | tf_op | source)
XLA Modules:
  0.0 294.4 jit_solution(14720587101093367091)
XLA Ops:
  7.2 0.7 all-gather.2.cloned.1.call-update
  7.9 2.4 stack.2
  10.3 14.6 %all-to-all-start = ((bf16[32,32,1024]{2,1,0:T(8,128)(2,1)}), bf16[32,32,1024]{2,1,0:T(8,128)(2,1)}, u32[]{:S(2)}, u32[]{:S(2)}) async-start(bf16[32,32,1024]{2,1,0:T(8,128)(2,1)} %stack.2), calls=%async_computation | async-start | bytes 4194304 | tf_op jit(solution)/shard_map/all_to_all | solution.py:101
  26.2 9.0 %reduce-window.19 = s32[32,8,128]{2,1,0:T(8,128)S(1)} reduce-window(s32[32,8,128]{2,1,0:T(8,128)S(1)} %fusion.39, s32[]{:T(128)} %constant.17.clone.1), window={size=1x1x128 pad=0_0x0_0x127_0}, to_apply=%region_6.7 | reduce-window | flops 4161536 | bytes 262148 | tf_op jit(solution)/shard_map/reduce-window.1
  35.6 1.3 dynamic-slice
  38.0 1.1 copy.41
  39.5 14.0 %all-reduce = s32[1024]{0:T(1024)S(1)} all-reduce(s32[1024]{0:T(1024)S(1)} %fusion.43), channel_id=1, replica_groups=mesh['blk'=16,'exp'=32] {'blk'}, use_global_device_ids=true, to_apply=%add | all-reduce | flops 1024 | bytes 8192
  54.9 2.0 select_reduce_fusion
  56.8 26.5 %all-gather.2.cloned.1.call-done = bf16[1,1024,1024]{2,1,0:T(8,128)(2,1)} async-done(((bf16[1,64,1024]{2,1,0:T(8,128)(2,1)}), bf16[1,1024,1024]{2,1,0:T(8,128)(2,1)}) %all-gather.2.cloned.1.call-update) | async-done | bytes 2097168 | tf_op jit(solution)/shard_map/all_gather | solution.py:88
  83.4 2.7 fusion.50
  86.0 1.3 copy.45
  87.4 1.5 copy.44
  88.9 2.9 %fusion = (f32[128,8,2]{0,2,1:T(2,128)S(1)}, f32[8,1024,128,2]{2,1,3,0:T(8,128)S(1)}) fusion(pred[1024]{0:T(1024)(128)(4,1)} %broadcast_compare_fusion, bf16[1024,8,64,1]{0,2,3,1:T(8,128)(2,1)S(1)} %bitcast.130, bf16[128,8,2,64]{0,3,2,1:T(8,128)(2,1)S(1)} %bitcast.133), kind=kOutput, calls=%fused_computation.5 | convolution fusion | flops 274724864 | bytes 9708544 | tf_op jit(solution)/shard_map/tkgd,skd->tkgs/dot_general | solution.py:35
  92.1 2.2 fusion.3
  94.3 1.5 fusion.17
  96.8 2.1 multiply_reduce_fusion
  99.1 7.1 %scatter_custom_fusion = bf16[1280,1024]{1,0:T(8,128)(2,1)} fusion(s32[1024]{0:T(1024)S(1)} %bitcast.144, bf16[]{:T(256)} %constant.12.clone.1, bf16[128,1024]{1,0:T(8,128)(2,1)S(1)} %multiply_convert_fusion), kind=kCustom, calls=%fused_computation.19 | custom fusion | bytes 2883586 | tf_op jit(solution)/shard_map/scatter | solution.py:118
  106.2 19.4 %all-to-all-start.1 = ((bf16[32,40,1024]{2,1,0:T(8,128)(2,1)}), bf16[32,40,1024]{2,1,0:T(8,128)(2,1)}, u32[]{:S(2)}, u32[]{:S(2)}) async-start(bf16[32,40,1024]{2,1,0:T(8,128)(2,1)} %bitcast.129), calls=%async_computation.1 | async-start | bytes 5242880 | tf_op jit(solution)/shard_map/all_to_all | solution.py:121
  125.9 0.9 broadcast_in_dim.91
  126.8 2.1 scatter_fusion
  128.9 57.8 %all-to-all-done.1 = bf16[32,40,1024]{2,1,0:T(8,128)(2,1)} async-done(((bf16[32,40,1024]{2,1,0:T(8,128)(2,1)}), bf16[32,40,1024]{2,1,0:T(8,128)(2,1)}, u32[]{:S(2)}, u32[]{:S(2)}) %all-to-all-start.1) | async-done | bytes 2621472 | tf_op jit(solution)/shard_map/all_to_all | solution.py:121
  186.7 3.9 %all-to-all-start.3 = ((bf16[32,8,1024]{2,1,0:T(8,128)(2,1)}), bf16[32,8,1024]{2,1,0:T(8,128)(2,1)S(1)}, u32[]{:S(2)}, u32[]{:S(2)}) async-start(bf16[32,8,1024]{2,1,0:T(8,128)(2,1)} %scatter_fusion), calls=%async_computation.3 | async-start | bytes 1048576 | tf_op jit(solution)/shard_map/all_to_all | solution.py:152
  190.6 4.7 %fusion.10 = f32[1280,1024]{1,0:T(8,128)S(1)} fusion(bf16[1280,1024]{1,0:T(8,128)(2,1)} %bitcast.33, bf16[1,1024,1024]{2,1,0:T(8,128)(2,1)S(1)} %copy-done), kind=kOutput, calls=%fused_computation.17 | convolution fusion | flops 2684354560 | bytes 9961472 | tf_op jit(solution)/shard_map/dot_general | solution.py:125
  195.4 3.1 %convolution_convert_fusion = bf16[1280,1024]{1,0:T(8,128)(2,1)} fusion(f32[1280,1024]{1,0:T(8,128)S(1)} %fusion.10, bf16[1,512,1024]{2,1,0:T(8,128)(2,1)S(1)} %copy-done.12), kind=kOutput, calls=%fused_computation.14 | convolution fusion | flops 1347420160 | bytes 8912896 | tf_op jit(solution)/shard_map/dot_general | solution.py:127
  198.5 5.3 %all-to-all-done.3 = bf16[32,8,1024]{2,1,0:T(8,128)(2,1)S(1)} async-done(((bf16[32,8,1024]{2,1,0:T(8,128)(2,1)}), bf16[32,8,1024]{2,1,0:T(8,128)(2,1)S(1)}, u32[]{:S(2)}, u32[]{:S(2)}) %all-to-all-start.3) | async-done | bytes 524320 | tf_op jit(solution)/shard_map/all_to_all | solution.py:152
  203.8 10.1 %all-to-all-start.2 = ((bf16[32,40,1024]{2,1,0:T(8,128)(2,1)}), bf16[32,40,1024]{2,1,0:T(8,128)(2,1)}, u32[]{:S(2)}, u32[]{:S(2)}) async-start(bf16[32,40,1024]{2,1,0:T(8,128)(2,1)} %bitcast.131), calls=%async_computation.2 | async-start | bytes 5242880 | tf_op jit(solution)/shard_map/all_to_all | solution.py:132
  214.0 0.9 copy.53
  214.9 60.0 %all-to-all-done.2 = bf16[32,40,1024]{2,1,0:T(8,128)(2,1)} async-done(((bf16[32,40,1024]{2,1,0:T(8,128)(2,1)}), bf16[32,40,1024]{2,1,0:T(8,128)(2,1)}, u32[]{:S(2)}, u32[]{:S(2)}) %all-to-all-start.2) | async-done | bytes 2621472 | tf_op jit(solution)/shard_map/all_to_all | solution.py:132
  274.9 8.1 %gather_fusion = bf16[1024,1024]{1,0:T(8,128)(2,1)} fusion(bf16[1280,1024]{1,0:T(8,128)(2,1)} %bitcast.37, s32[1024]{0:T(1024)S(1)} %broadcast_clamp_fusion), kind=kCustom, calls=%fused_computation | custom fusion | bytes 4198400 | tf_op jit(solution)/shard_map/gather | solution.py:134
  283.0 2.9 fusion.5
  286.0 0.8 fusion.35
  286.7 0.8 copy.66
  (71 shorter events, 4.8 us)
Async XLA Ops:
  7.2 183.4 %copy-start = (bf16[1,1024,1024]{2,1,0:T(8,128)(2,1)S(1)}, bf16[1,1024,1024]{2,1,0:T(8,128)(2,1)}, u32[]{:S(2)}) copy-start(bf16[1,1024,1024]{2,1,0:T(8,128)(2,1)} %param.23) | copy-start | bytes 6291460
  7.2 76.2 %all-gather.2.cloned.1.call-start = ((), (), s32[]{:S(2)}) async-start(), calls=%async_computation.4 | async-start | bytes 2228224 | tf_op jit(solution)/shard_map/all_gather | solution.py:88
  10.3 14.7 %copy-start.13 = (s32[1,2]{1,0:T(1,128)S(1)}, s32[1,2]{1,0:T(1,128)}, u32[]{:S(2)}) copy-start(s32[1,2]{1,0:T(1,128)} %param.18) | copy-start | bytes 28
  10.3 15.5 %copy-start.7 = (s32[1,128,8]{1,2,0:T(8,128)S(1)}, s32[1,128,8]{1,2,0:T(8,128)}, u32[]{:S(2)}) copy-start(s32[1,128,8]{1,2,0:T(8,128)} %param.21) | copy-start | bytes 12292
  10.3 15.7 %copy-start.14 = (s32[1,1,4]{2,1,0:T(1,128)S(1)}, s32[1,1,4]{2,1,0:T(1,128)}, u32[]{:S(2)}) copy-start(s32[1,1,4]{2,1,0:T(1,128)} %param.19) | copy-start | bytes 52
  10.3 27.4 %copy-start.4 = (bf16[1,128,1024]{2,1,0:T(8,128)(2,1)S(1)}, bf16[1,128,1024]{2,1,0:T(8,128)(2,1)}, u32[]{:S(2)}) copy-start(bf16[1,128,1024]{2,1,0:T(8,128)(2,1)} %param.15) | copy-start | bytes 786436
  10.3 85.9 %all-to-all-start = ((bf16[32,32,1024]{2,1,0:T(8,128)(2,1)}), bf16[32,32,1024]{2,1,0:T(8,128)(2,1)}, u32[]{:S(2)}, u32[]{:S(2)}) async-start(bf16[32,32,1024]{2,1,0:T(8,128)(2,1)} %stack.2), calls=%async_computation | async-start | bytes 4194304 | tf_op jit(solution)/shard_map/all_to_all | solution.py:101
  88.8 3.0 %copy-start.6 = (f32[128,8,2]{0,2,1:T(2,128)S(1)}, f32[128,8,2]{0,2,1:T(2,128)}, u32[]{:S(2)}) copy-start(f32[128,8,2]{0,2,1:T(2,128)} %get-tuple-element.21) | copy-start | bytes 24580
  88.9 3.0 %copy-start.1 = (f32[128,8,2,128]{0,3,2,1:T(8,128)S(1)}, f32[128,8,2,128]{0,3,2,1:T(8,128)}, u32[]{:S(2)}) copy-start(f32[128,8,2,128]{0,3,2,1:T(8,128)} %get-tuple-element.22) | copy-start | bytes 3145732
  88.9 3.2 %copy-start.9 = (pred[1024]{0:T(1024)(128)(4,1)S(1)}, pred[1024]{0:T(1024)(128)(4,1)}, u32[]{:S(2)}) copy-start(pred[1024]{0:T(1024)(128)(4,1)} %broadcast_compare_fusion) | copy-start | bytes 3076
  92.1 2.2 copy-start.2
  95.9 1.0 copy-start.5
  96.2 2.9 copy-start.8
  106.2 19.4 %copy-start.11 = (s32[1,8,1]{1,2,0:T(1,128)S(1)}, s32[1,8,1]{1,2,0:T(1,128)}, u32[]{:S(2)}) copy-start(s32[1,8,1]{1,2,0:T(1,128)} %param.25) | copy-start | bytes 100
  106.2 20.6 %copy-start.3 = (bf16[1,64,1024]{2,1,0:T(8,128)(2,1)S(1)}, bf16[1,64,1024]{2,1,0:T(8,128)(2,1)}, u32[]{:S(2)}) copy-start(bf16[1,64,1024]{2,1,0:T(8,128)(2,1)} %param.16) | copy-start | bytes 393220
  106.2 80.4 %all-to-all-start.1 = ((bf16[32,40,1024]{2,1,0:T(8,128)(2,1)}), bf16[32,40,1024]{2,1,0:T(8,128)(2,1)}, u32[]{:S(2)}, u32[]{:S(2)}) async-start(bf16[32,40,1024]{2,1,0:T(8,128)(2,1)} %bitcast.129), calls=%async_computation.1 | async-start | bytes 5242880 | tf_op jit(solution)/shard_map/all_to_all | solution.py:121
  186.7 17.1 %all-to-all-start.3 = ((bf16[32,8,1024]{2,1,0:T(8,128)(2,1)}), bf16[32,8,1024]{2,1,0:T(8,128)(2,1)S(1)}, u32[]{:S(2)}, u32[]{:S(2)}) async-start(bf16[32,8,1024]{2,1,0:T(8,128)(2,1)} %scatter_fusion), calls=%async_computation.3 | async-start | bytes 1048576 | tf_op jit(solution)/shard_map/all_to_all | solution.py:152
  190.6 4.8 %copy-start.12 = (bf16[1,512,1024]{2,1,0:T(8,128)(2,1)S(1)}, bf16[1,512,1024]{2,1,0:T(8,128)(2,1)}, u32[]{:S(2)}) copy-start(bf16[1,512,1024]{2,1,0:T(8,128)(2,1)} %param.24) | copy-start | bytes 3145732
  203.8 10.1 %copy-start.10 = (f32[1,128,8]{1,2,0:T(8,128)S(1)}, f32[1,128,8]{1,2,0:T(8,128)}, u32[]{:S(2)}) copy-start(f32[1,128,8]{1,2,0:T(8,128)} %param.22) | copy-start | bytes 12292
  203.8 71.1 %all-to-all-start.2 = ((bf16[32,40,1024]{2,1,0:T(8,128)(2,1)}), bf16[32,40,1024]{2,1,0:T(8,128)(2,1)}, u32[]{:S(2)}, u32[]{:S(2)}) async-start(bf16[32,40,1024]{2,1,0:T(8,128)(2,1)} %bitcast.131), calls=%async_computation.2 | async-start | bytes 5242880 | tf_op jit(solution)/shard_map/all_to_all | solution.py:132
Sparse Core Ops, SparseCore 0:
  10.1 73.2 all-gather.1
